TPU v7x, 32 devices: a whole 2x2x4 slice. The times are simulated.
32 devices in a mesh: ctx: 4 (over z), fsdp: 2 (over y), rep: 4 (over x, core).
Axes of the slice: x: 2, y: 2, z: 4, core: 2. Of those that a mesh axis runs over, the one named last changes fastest.
Arguments:
- frames_in: bfloat16 [8, 512, 1024], P('rep', 'ctx', 'fsdp'), parts along dimension 0, may hold values from -6 to 6
- lengths: int32 [8], P('rep'), parts along dimension 0, may hold values from 128 to 512, as said below
- conv_weight: bfloat16 [16, 128, 64, 64], P('fsdp'), may hold values from -0.0625 to 0.0625
- conv_bias: bfloat16 [1024], P('fsdp'), may hold values from -3 to 3
- norm_gain: float32 [1024], replicated, may hold values from 0.1 to 1.9
- norm_shift: float32 [1024], replicated, may hold values from -3 to 3
- w_query: bfloat16 [1024, 512], replicated
- w_key: bfloat16 [1024, 512], replicated
- w_value: bfloat16 [1024, 512], replicated, may hold values from -0.1875 to 0.1875
Outputs:
- hidden: bfloat16 [8, 512, 1024], P('rep', 'ctx', 'fsdp'), parts along dimension 0
- context: bfloat16 [8, 512, 512], P(('rep', 'fsdp'), 'ctx'), parts along dimension 0
There are 4 independent parts, one for each index of `rep`. A program takes and returns all parts, laid end to end along the dimension named above; an argument that names none is the same for every part. Nothing has to cross between parts.
Inputs may be any that keep to these rules, and one draw needn't show every extreme that they name: `lengths`: one recording in every draw has all 512 frames live.
All inputs are finite; a program needn't handle non-finite values.
Results may differ from a plain program's by a relative error of at most 0.012.
Values may be sent and summed in bfloat16 or wider, within the bound.
No kernel may reach another device: no remote copies, remote signals or barrier semaphores. Data moves between devices by JAX's collectives and lax.ppermute only.
A program may use at most 128 MiB of HBM per device.

v0:
```python
import math
import jax
import jax.numpy as jnp
from jax import lax
from jax.sharding import PartitionSpec as P

HD = 64


def padded_2(x, sides, width):
    for axis, dim in sides:
        size, length = (lax.axis_size(axis), x.shape[dim])
        up = [(i, (i + 1) % size) for i in range(size - 1)]
        down = [(j, i) for i, j in up]
        last = lax.slice_in_dim(x, length - width, length, axis=dim)
        first = lax.slice_in_dim(x, 0, width, axis=dim)
        before = lax.ppermute(last, axis, up)
        after = lax.ppermute(first, axis, down)
        x = jnp.concatenate([before, x, after], axis=dim)
    return x


def attend(carry, piece, start, queries, own_length):
    best, total, accum = carry
    keys_part, vals_part = piece
    count = keys_part.shape[0]
    head_count = queries.shape[1]
    keys_part = keys_part.reshape(count, head_count, HD)
    vals_part = vals_part.reshape(count, head_count, HD)
    scores = jnp.einsum(
        "fhd,nhd->fhn", queries, keys_part, preferred_element_type=jnp.float32
    ) / math.sqrt(HD)
    valid = (start + jnp.arange(count, dtype=jnp.int32) < own_length)[None, None, :]
    scores = jnp.where(valid, scores, -1e30)
    fresh = jnp.maximum(best, jnp.max(scores, axis=2))
    weights = jnp.where(valid, jnp.exp(scores - fresh[:, :, None]), 0.0)
    factor = jnp.exp(best - fresh)
    total = total * factor + jnp.sum(weights, axis=2)
    accum = accum * factor[:, :, None] + jnp.einsum(
        "fhn,nhd->fhd", weights.astype(jnp.bfloat16), vals_part, preferred_element_type=jnp.float32
    )
    return (fresh, total, accum)


def start_state(rows, heads_here):
    return (
        jnp.full((rows, heads_here), -1e30, jnp.float32),
        jnp.zeros((rows, heads_here), jnp.float32),
        jnp.zeros((rows, heads_here, HD), jnp.float32),
    )


def blockwise(carry, all_keys, all_vals, queries, own_length, block_rows):
    block_count = all_keys.shape[0] // block_rows

    def block_step(state, index):
        begin = index * block_rows
        piece = (
            lax.dynamic_slice_in_dim(all_keys, begin, block_rows, 0),
            lax.dynamic_slice_in_dim(all_vals, begin, block_rows, 0),
        )
        return (attend(state, piece, begin, queries, own_length), None)

    final, unused = lax.scan(block_step, carry, jnp.arange(block_count, dtype=jnp.int32))
    return final


def finish(final, query_pos, own_length):
    best, total, accum = final
    result = accum / total[:, :, None]
    query_live = (query_pos < own_length)[:, None, None]
    result = jnp.where(query_live, result, 0.0)
    return result.reshape(result.shape[0], result.shape[1] * HD).astype(jnp.bfloat16)


def per_device(
    frames_in, lengths, conv_weight, conv_bias, norm_gain, norm_shift, w_query, w_key, w_value
):
    record_count, frame_rows, channels = frames_in.shape
    ctx_place = lax.axis_index("ctx")
    positions = ctx_place * frame_rows + jnp.arange(frame_rows, dtype=jnp.int32)
    live = positions[None, :] < lengths[:, None]
    masked = jnp.where(live[:, :, None], frames_in, jnp.zeros((), frames_in.dtype))
    groups_here, kernel_width, group_in, group_out = conv_weight.shape
    half_width = kernel_width // 2
    padded = padded_2(masked, (("ctx", 1),), half_width)
    kernel = conv_weight.transpose(1, 2, 0, 3).reshape(
        kernel_width, group_in, groups_here * group_out
    )
    conv_out = lax.conv_general_dilated(
        padded[:, : frame_rows + kernel_width - 1],
        kernel,
        (1,),
        "VALID",
        dimension_numbers=("NWC", "WIO", "NWC"),
        feature_group_count=groups_here,
        preferred_element_type=jnp.float32,
    )
    hidden = (
        masked.astype(jnp.float32)
        + jax.nn.gelu(conv_out + conv_bias.astype(jnp.float32), approximate=False)
    ).astype(jnp.bfloat16)
    record = lax.all_to_all(hidden, "fsdp", split_axis=0, concat_axis=2, tiled=True)
    own_length = lax.dynamic_index_in_dim(lengths, lax.axis_index("fsdp"), 0, keepdims=False)
    flat = record[0].astype(jnp.float32)
    centre = jnp.mean(flat, axis=1, keepdims=True)
    spread = jnp.mean((flat - centre) ** 2, axis=1, keepdims=True)
    normed = ((flat - centre) / jnp.sqrt(spread + 1e-05) * norm_gain + norm_shift).astype(
        jnp.bfloat16
    )
    query_flat = jnp.dot(normed, w_query, preferred_element_type=jnp.float32).astype(jnp.bfloat16)
    key_flat = jnp.dot(normed, w_key, preferred_element_type=jnp.float32).astype(jnp.bfloat16)
    val_flat = jnp.dot(normed, w_value, preferred_element_type=jnp.float32).astype(jnp.bfloat16)
    head_count = query_flat.shape[1] // HD
    queries = query_flat.reshape(frame_rows, head_count, HD)
    block_rows = 4 * frame_rows
    both = lax.all_gather(jnp.concatenate([key_flat, val_flat], axis=1), "ctx", axis=0, tiled=True)
    whole_keys, whole_vals = (both[:, : key_flat.shape[1]], both[:, key_flat.shape[1] :])
    final = blockwise(
        start_state(frame_rows, head_count), whole_keys, whole_vals, queries, own_length, block_rows
    )
    result = finish(final, positions, own_length).reshape(1, frame_rows, head_count * HD)
    return (hidden, result)


def solution(mesh):
    in_specs = (
        P("rep", "ctx", "fsdp"),
        P("rep"),
        P("fsdp", None, None, None),
        P("fsdp"),
        P(),
        P(),
        P(),
        P(),
        P(),
    )
    out_specs = (P("rep", "ctx", "fsdp"), P(("rep", "fsdp"), "ctx", None))
    return jax.shard_map(
        per_device, mesh=mesh, in_specs=in_specs, out_specs=out_specs, check_vma=False
    )
```

profile of v0, /device:TPU:0, one launch (start us, length us, event | category | flops | bytes accessed | tf_op | source)
XLA Modules:
  0.0 142.5 jit_solution(2669789858870461635)
XLA Ops:
  7.2 0.0 copy-start
  7.2 0.0 all-gather.2.cloned.1.call-start
  7.2 1.2 copy.17
  8.4 0.0 copy-start.1
  8.5 0.8 broadcast_compare_fusion
  9.2 0.5 copy-done.8
  9.8 0.1 fusion.36
  9.9 4.9 %collective-permute-start = (bf16[2,64,512]{1,2,0:T(8,128)(2,1)S(1)}, bf16[2,64,512]{1,2,0:T(8,128)(2,1)S(1)}, u32[]{:S(2)}, u32[]{:S(2)}) collective-permute-start(bf16[2,64,512]{1,2,0:T(8,128)(2,1)S(1)} %get-tuple-element.32), channel_id=1, source_target_pairs={{0,8},{8,16},{16,24},{1,9},{9,17},{17,25},{2,10},{10,18},{18,26},{... | collective-permute-start | bytes 393224 | tf_op jit(solution)/shard_map/ppermute | solution.py:17
  14.8 0.0 copy-start.10
  14.9 1.3 collective-permute-start.1
  16.2 24.0 %copy.19 = bf16[8,128,64,64]{3,2,0,1:T(8,128)(2,1)} copy(bf16[8,128,64,64]{1,3,2,0:T(8,128)(2,1)} %param.11) | data formatting | bytes 16777216 | tf_op args[2]
  40.1 0.0 copy-done.10
  40.1 0.6 convert_element_type.59
  40.7 0.0 collective-permute-done
  40.7 0.0 collective-permute-done.1
  40.7 0.3 pad_maximum_fusion
  41.1 2.1 %copy.18 = bf16[2,255,8,64]{3,0,2,1:T(2,128)(2,1)} copy(bf16[2,255,8,64]{1,3,2,0:T(8,128)(2,1)S(1)} %bitcast.62) | data formatting | bytes 1044480 | tf_op jit(solution)/shard_map/slice | solution.py:91
  43.2 41.1 %fusion.37 = f32[2,128,8,64]{3,0,2,1:T(2,128)S(1)} fusion(bf16[2,255,8,64]{3,0,2,1:T(2,128)(2,1)} %copy.18, bf16[8,128,64,64]{3,2,0,1:T(8,128)(2,1)} %copy.19), kind=kOutput, calls=%fused_computation.68 | convolution fusion | flops 2147483648 | bytes 9435136 | tf_op jit(solution)/shard_map/conv_general_dilated | solution.py:90
  84.2 0.0 copy-start.6
  84.3 0.0 copy-start.7
  84.3 0.7 copy.20
  85.0 0.0 copy-start.3
  85.0 1.3 fusion.17
  86.3 7.8 %all_to_all.4 = bf16[2,128,512]{1,2,0:T(8,128)(2,1)S(1)} all-to-all(bf16[2,128,512]{1,2,0:T(8,128)(2,1)S(1)} %fusion.17), channel_id=1, replica_groups=mesh['ctx'=4,'fsdp'=2,'rep'=4] {'fsdp'}, dimensions={0} | all-to-all | bytes 524288 | tf_op jit(solution)/shard_map/all_to_all | solution.py:103
  94.1 0.2 convert_reduce_fusion
  94.2 0.2 fusion.22
  94.4 0.0 copy-start.11
  94.4 0.3 fusion.29
  94.8 0.0 copy-start.4
  94.8 0.3 convolution_convert_fusion.1
  95.1 0.0 copy-done.3
  95.1 0.3 convolution_convert_fusion.2
  95.5 0.7 pad_maximum_fusion.2
  96.2 0.0 all-gather.2.cloned.1.call-update
  96.3 0.6 dynamic_slice.11
  96.8 0.6 iota_compare_fusion
  97.5 0.7 broadcast_compare_fusion.1
  98.2 0.9 copy.25
  99.0 0.3 convolution_convert_fusion
  99.4 0.1 copy.22
  99.5 26.2 %all-gather.2.cloned.1.call-done = bf16[512,1024]{1,0:T(8,128)(2,1)} async-done(((bf16[128,1024]{1,0:T(8,128)(2,1)}), bf16[512,1024]{1,0:T(8,128)(2,1)}) %all-gather.2.cloned.1.call-update) | async-done | bytes 1048592 | tf_op jit(solution)/shard_map/all_gather | solution.py:117
  125.7 2.1 %fusion.35 = (bf16[512,512]{1,0:T(8,128)(2,1)S(1)}, bf16[512,512]{1,0:T(8,128)(2,1)}) fusion(bf16[512,1024]{1,0:T(8,128)(2,1)} %all-gather.2.cloned.1.call-done), kind=kLoop, calls=%fused_computation.66 | loop fusion | bytes 2097152 | tf_op jit(solution)/shard_map/slice | solution.py:118
  127.8 1.0 copy.21
  128.8 1.7 %bitcast_reduce_fusion = (f32[128,8]{0,1:T(8,128)S(1)}, f32[8,512,128]{2,1,0:T(8,128)S(1)}) fusion(pred[512]{0:T(512)(128)(4,1)S(1)} %iota_compare_fusion, bf16[512,8,64]{0,2,1:T(8,128)(2,1)} %bitcast.63, bf16[128,8,64]{0,2,1:T(8,128)(2,1)S(1)} %bitcast.64), kind=kOutput, calls=%fused_computation.1 | convolution fusion | flops 68680704 | bytes 2757120 | tf_op jit(solution)/shard_map/while/body/eval_jaxpr/fhd,nhd->fhn/dot_general | solution.py:30
  130.5 0.6 fusion.2
  131.1 2.1 %copy.23 = bf16[512,512]{0,1:T(8,128)(2,1)} copy(bf16[512,512]{1,0:T(8,128)(2,1)} %get-tuple-element.23) | data formatting | bytes 1048576 | tf_op jit(solution)/shard_map/slice | solution.py:118
  133.1 1.8 %fusion.7 = bf16[128,8,64]{0,2,1:T(8,128)(2,1)S(1)} fusion(bf16[512,8,64]{0,2,1:T(8,128)(2,1)} %bitcast.65, f32[8,512,128]{2,1,0:T(8,128)S(1)} %get-tuple-element.37, f32[128,8]{0,1:T(8,128)S(1)} %broadcast_maximum_fusion, pred[512]{0:T(512)(128)(4,1)S(1)} %iota_compare_fusion, f32[128,8]{0,1:T(8,128)S(1)} %get-tuple-element.35, ...), kind=kOutput, calls=%fused_computation.11 | convolution fusion | flops 69992448 | bytes 2765440 | tf_op jit(solution)/shard_map/while/body/eval_jaxpr/fhn,nhd->fhd/dot_general | solution.py:39
  134.9 0.8 copy.26
  (19 shorter events, 0.1 us)
Async XLA Ops:
  7.2 87.6 %copy-start = (bf16[1024,512]{1,0:T(8,128)(2,1)S(1)}, bf16[1024,512]{1,0:T(8,128)(2,1)}, u32[]{:S(2)}) copy-start(bf16[1024,512]{1,0:T(8,128)(2,1)} %param.17) | copy-start | bytes 3145732
  7.2 118.5 %all-gather.2.cloned.1.call-start = ((), (), s32[]{:S(2)}) async-start(), calls=%async_computation.1 | async-start | bytes 1310720 | tf_op jit(solution)/shard_map/all_gather | solution.py:117
  8.4 31.7 %copy-start.1 = (bf16[2,128,512]{1,2,0:T(8,128)(2,1)}, bf16[2,128,512]{1,2,0:T(8,128)(2,1)S(1)}, u32[]{:S(2)}) copy-start(bf16[2,128,512]{1,2,0:T(8,128)(2,1)S(1)} %copy.17) | copy-start | bytes 786436
  9.2 0.5 copy-start.8
  9.9 30.8 %collective-permute-start = (bf16[2,64,512]{1,2,0:T(8,128)(2,1)S(1)}, bf16[2,64,512]{1,2,0:T(8,128)(2,1)S(1)}, u32[]{:S(2)}, u32[]{:S(2)}) collective-permute-start(bf16[2,64,512]{1,2,0:T(8,128)(2,1)S(1)} %get-tuple-element.32), channel_id=1, source_target_pairs={{0,8},{8,16},{16,24},{1,9},{9,17},{17,25},{2,10},{10,18},{18,26},{... | collective-permute-start | bytes 393224 | tf_op jit(solution)/shard_map/ppermute | solution.py:17
  14.8 25.3 %copy-start.10 = (bf16[512]{0:T(512)(128)(2,1)S(1)}, bf16[512]{0:T(512)(128)(2,1)}, u32[]{:S(2)}) copy-start(bf16[512]{0:T(512)(128)(2,1)} %param.12) | copy-start | bytes 3076
  14.9 25.9 %collective-permute-start.1 = (bf16[2,64,512]{1,2,0:T(8,128)(2,1)S(1)}, bf16[2,64,512]{1,2,0:T(8,128)(2,1)S(1)}, u32[]{:S(2)}, u32[]{:S(2)}) collective-permute-start(bf16[2,64,512]{1,2,0:T(8,128)(2,1)S(1)} %get-tuple-element.33), channel_id=1, source_target_pairs={{8,0},{16,8},{24,16},{9,1},{17,9},{25,17},{10,2},{18,10},{26,18},{... | collective-permute-start | bytes 393224 | tf_op jit(solution)/shard_map/ppermute | solution.py:18
  43.2 41.8 %copy-start.2 = (bf16[2,128,512]{1,2,0:T(8,128)(2,1)S(1)}, bf16[2,128,512]{1,2,0:T(8,128)(2,1)}, u32[]{:S(2)}) copy-start(bf16[2,128,512]{1,2,0:T(8,128)(2,1)} %copy-done.1) | copy-start | bytes 786436
  43.2 41.8 %copy-start.5 = (f32[512]{0:T(512)S(1)}, f32[512]{0:T(512)}, u32[]{:S(2)}) copy-start(f32[512]{0:T(512)} %convert_element_type.59) | copy-start | bytes 6148
  43.2 41.9 %copy-start.9 = (pred[2,128]{1,0:T(4,128)(4,1)S(1)}, pred[2,128]{1,0:T(4,128)(4,1)}, u32[]{:S(2)}) copy-start(pred[2,128]{1,0:T(4,128)(4,1)} %copy-done.8) | copy-start | bytes 772
  84.2 10.1 %copy-start.6 = (f32[1024]{0:T(1024)S(1)}, f32[1024]{0:T(1024)}, u32[]{:S(2)}) copy-start(f32[1024]{0:T(1024)} %param.14) | copy-start | bytes 12292
  84.3 10.1 %copy-start.7 = (f32[1024]{0:T(1024)S(1)}, f32[1024]{0:T(1024)}, u32[]{:S(2)}) copy-start(f32[1024]{0:T(1024)} %param.13) | copy-start | bytes 12292
  85.0 10.1 %copy-start.3 = (bf16[1024,512]{1,0:T(8,128)(2,1)S(1)}, bf16[1024,512]{1,0:T(8,128)(2,1)}, u32[]{:S(2)}) copy-start(bf16[1024,512]{1,0:T(8,128)(2,1)} %param.16) | copy-start | bytes 3145732
  94.4 1.9 %copy-start.11 = (s32[2]{0:T(128)S(1)}, s32[2]{0:T(128)}, u32[]{:S(2)}) copy-start(s32[2]{0:T(128)} %param.10) | copy-start | bytes 28
  94.8 4.3 %copy-start.4 = (bf16[1024,512]{1,0:T(8,128)(2,1)S(1)}, bf16[1024,512]{1,0:T(8,128)(2,1)}, u32[]{:S(2)}) copy-start(bf16[1024,512]{1,0:T(8,128)(2,1)} %param.15) | copy-start | bytes 3145732
Sparse Core Ops, SparseCore 0:
  96.4 29.2 all-gather.1
where the time goes:
time: 143 us
  matrix products  45.5 us (32%)
  local copies, waits for them, and re-layouts  36.2 us (25%)
  waiting for transfers between devices  26.2 us (18%)
  between operations  14.3 us (10%)
  blocking collectives  7.76 us (5%)
  starting transfers between devices  6.27 us (4%)
  other arithmetic  6.24 us (4%)
    conv_general_dilated x1, matrix products, per_device(): lax.conv_general_dilated(padded[:, :frame_rows + kernel_width - 1], kerne...  41.1 us
    unnamed x28, local copies, waits for them, and re-layouts  27.4 us
    all_gather x1, waiting for transfers between devices, per_device(): lax.all_gather(jnp.concatenate([key_flat, val_flat], axis=1), 'ctx', axis...  26.2 us
    all_to_all x1, blocking collectives, per_device(): lax.all_to_all(hidden, 'fsdp', split_axis=0, concat_axis=2, tiled=True)  7.76 us
    ppermute x1, starting transfers between devices, padded_2(): before = lax.ppermute(last, axis, up)  4.94 us
    slice x2, local copies, waits for them, and re-layouts, per_device(): both[:, :key_flat.shape[1]]  3.1 us
  transfers between devices with their start and end apart: 3, of which 1 were waited for; matrix products, arithmetic and copies ran while one was open for 19% of the time, Pallas kernels for 0%

commit v1 on v0

--- a/solution.py
+++ b/solution.py
@@ -5,6 +5,19 @@
 from jax.sharding import PartitionSpec as P
 
 HD = 64
+
+
+def ring_gather(value, axis, dim):
+    ways = lax.axis_size(axis)
+    up = [(d, (d + 1) % ways) for d in range(ways)]
+    down = [(d, (d - 1) % ways) for d in range(ways)]
+    earlier, later = ([value], [value])
+    for _ in range(ways // 2):
+        earlier.append(lax.ppermute(earlier[-1], axis, up))
+    for _ in range((ways - 1) // 2):
+        later.append(lax.ppermute(later[-1], axis, down))
+    line = jnp.concatenate([*earlier[::-1], *later[1:]], axis=dim)
+    return jnp.roll(line, (lax.axis_index(axis) - ways // 2) * value.shape[dim], axis=dim)
 
 
 def padded_2(x, sides, width):
@@ -114,7 +127,7 @@
     head_count = query_flat.shape[1] // HD
     queries = query_flat.reshape(frame_rows, head_count, HD)
     block_rows = 4 * frame_rows
-    both = lax.all_gather(jnp.concatenate([key_flat, val_flat], axis=1), "ctx", axis=0, tiled=True)
+    both = ring_gather(jnp.concatenate([key_flat, val_flat], axis=1), "ctx", 0)
     whole_keys, whole_vals = (both[:, : key_flat.shape[1]], both[:, key_flat.shape[1] :])
     final = blockwise(
         start_state(frame_rows, head_count), whole_keys, whole_vals, queries, own_length, block_rows

time: 143 us -> 120 us (0.84)
  waiting for transfers between devices: 26.2 us -> 10.3 us
  between operations: 14.3 us -> 1 us
  starting transfers between devices: 6.27 us -> 12.8 us
    all_gather x1 -> x0, waiting for transfers between devices: 26.2 us -> none  [per_device(): lax.all_gather(jnp.concatenate([key_flat, val_flat], axis=1), 'ctx', axis...]
    ppermute x0 -> x3, waiting for transfers between devices: none -> 10.3 us  [the longest x2 7.83 us: ring_gather(): earlier.append(lax.ppermute(earlier[-1], axis, up))]
    ppermute x0 -> x3, starting transfers between devices: none -> 6.53 us  [the longest x1 3.82 us: ring_gather(): later.append(lax.ppermute(later[-1], axis, down))]
    unnamed x28 -> x35, local copies, waits for them, and re-layouts: 27.4 us -> 27.5 us
  transfers between devices with their start and end apart: 3 -> 5, of which waited for: 1 -> 3; matrix products, arithmetic and copies ran while one was open for 19% -> 25% of each run, Pallas kernels for 0% -> 0%
where the time goes in v1:
time: 120 us
  matrix products  46.2 us (38%)
  local copies, waits for them, and re-layouts  36 us (30%)
  starting transfers between devices  12.8 us (11%)
  waiting for transfers between devices  10.3 us (9%)
  blocking collectives  7.76 us (6%)
  other arithmetic  5.56 us (5%)
    conv_general_dilated x1, matrix products, per_device(): lax.conv_general_dilated(padded[:, :frame_rows + kernel_width - 1], kerne...  41.1 us
    unnamed x35, local copies, waits for them, and re-layouts  27.5 us
    ppermute x2, waiting for transfers between devices, ring_gather(): earlier.append(lax.ppermute(earlier[-1], axis, up))  7.83 us
    all_to_all x1, blocking collectives, per_device(): lax.all_to_all(hidden, 'fsdp', split_axis=0, concat_axis=2, tiled=True)  7.76 us
    ppermute x1, starting transfers between devices, padded_2(): before = lax.ppermute(last, axis, up)  4.94 us
    ppermute x1, starting transfers between devices, ring_gather(): later.append(lax.ppermute(later[-1], axis, down))  3.82 us
    ppermute x2, starting transfers between devices, ring_gather(): earlier.append(lax.ppermute(earlier[-1], axis, up))  2.71 us
    ppermute x1, waiting for transfers between devices, ring_gather(): later.append(lax.ppermute(later[-1], axis, down))  2.48 us
  transfers between devices with their start and end apart: 5, of which 3 were waited for; matrix products, arithmetic and copies ran while one was open for 25% of the time, Pallas kernels for 0%

profile of v1, /device:TPU:0, one launch (start us, length us, event | category | flops | bytes accessed | tf_op | source)
XLA Modules:
  0.0 119.6 jit_solution(3163766439176948879)
XLA Ops:
  0.6 0.0 copy-start
  0.7 1.2 %copy.17 = bf16[2,128,512]{1,2,0:T(8,128)(2,1)S(1)} copy(bf16[2,128,512]{2,1,0:T(8,128)(2,1)} %param.9) | data formatting | bytes 524288 | tf_op args[0]
  1.9 0.0 copy-start.1
  1.9 0.8 broadcast_compare_fusion
  2.6 0.6 copy-done.9
  3.2 0.1 fusion.35
  3.4 4.9 %collective-permute-start = (bf16[2,64,512]{1,2,0:T(8,128)(2,1)S(1)}, bf16[2,64,512]{1,2,0:T(8,128)(2,1)S(1)}, u32[]{:S(2)}, u32[]{:S(2)}) collective-permute-start(bf16[2,64,512]{1,2,0:T(8,128)(2,1)S(1)} %get-tuple-element.32), channel_id=1, source_target_pairs={{0,8},{8,16},{16,24},{1,9},{9,17},{17,25},{2,10},{10,18},{18,26},{... | collective-permute-start | bytes 393224 | tf_op jit(solution)/shard_map/ppermute | solution.py:30
  8.3 0.0 copy-start.11
  8.3 1.3 %collective-permute-start.1 = (bf16[2,64,512]{1,2,0:T(8,128)(2,1)S(1)}, bf16[2,64,512]{1,2,0:T(8,128)(2,1)S(1)}, u32[]{:S(2)}, u32[]{:S(2)}) collective-permute-start(bf16[2,64,512]{1,2,0:T(8,128)(2,1)S(1)} %get-tuple-element.33), channel_id=1, source_target_pairs={{8,0},{16,8},{24,16},{9,1},{17,9},{25,17},{10,2},{18,10},{26,18},{... | collective-permute-start | bytes 393224 | tf_op jit(solution)/shard_map/ppermute | solution.py:31
  9.6 23.9 %copy.19 = bf16[8,128,64,64]{3,2,0,1:T(8,128)(2,1)} copy(bf16[8,128,64,64]{1,3,2,0:T(8,128)(2,1)} %param.11) | data formatting | bytes 16777216 | tf_op args[2]
  33.6 0.0 copy-done.11
  33.6 0.6 convert_element_type.59
  34.2 0.0 collective-permute-done
  34.2 0.0 collective-permute-done.1
  34.2 0.3 pad_maximum_fusion
  34.5 2.1 %copy.18 = bf16[2,255,8,64]{3,0,2,1:T(2,128)(2,1)} copy(bf16[2,255,8,64]{1,3,2,0:T(8,128)(2,1)S(1)} %bitcast.62) | data formatting | bytes 1044480 | tf_op jit(solution)/shard_map/slice | solution.py:104
  36.6 41.1 %fusion.36 = f32[2,128,8,64]{3,0,2,1:T(2,128)S(1)} fusion(bf16[2,255,8,64]{3,0,2,1:T(2,128)(2,1)} %copy.18, bf16[8,128,64,64]{3,2,0,1:T(8,128)(2,1)} %copy.19), kind=kOutput, calls=%fused_computation.76 | convolution fusion | flops 2147483648 | bytes 9435136 | tf_op jit(solution)/shard_map/conv_general_dilated | solution.py:103
  77.7 0.0 copy-start.7
  77.7 0.0 copy-start.8
  77.7 0.7 copy.20
  78.5 0.0 copy-start.3
  78.5 1.3 %fusion.17 = bf16[2,128,512]{1,2,0:T(8,128)(2,1)S(1)} fusion(f32[2,128,8,64]{1,3,2,0:T(8,128)S(1)} %copy.20, f32[512]{0:T(512)S(1)} %copy-done.6, bf16[2,128,512]{1,2,0:T(8,128)(2,1)S(1)} %copy-done.2, pred[2,128]{1,0:T(4,128)(4,1)S(1)} %copy-done.10), kind=kLoop, calls=%fused_computation.24 | loop fusion | flops 9043968 | bytes 1050880 | tf_op jit(solution)/shard_map/convert_element_type | solution.py:115
  79.7 7.8 %all_to_all.4 = bf16[2,128,512]{1,2,0:T(8,128)(2,1)S(1)} all-to-all(bf16[2,128,512]{1,2,0:T(8,128)(2,1)S(1)} %fusion.17), channel_id=1, replica_groups=mesh['ctx'=4,'fsdp'=2,'rep'=4] {'fsdp'}, dimensions={0} | all-to-all | bytes 524288 | tf_op jit(solution)/shard_map/all_to_all | solution.py:116
  87.5 0.2 convert_reduce_fusion
  87.7 0.2 fusion.22
  87.8 0.3 fusion.29
  88.2 0.0 copy-start.4
  88.2 0.3 convolution_convert_fusion.1
  88.6 0.3 convolution_convert_fusion.2
  88.9 2.7 %collective-permute-start.2 = (bf16[128,1024]{1,0:T(8,128)(2,1)S(1)}, bf16[128,1024]{1,0:T(8,128)(2,1)S(1)}, u32[]{:S(2)}, u32[]{:S(2)}) collective-permute-start(bf16[128,1024]{1,0:T(8,128)(2,1)S(1)} %pad_maximum_fusion.2), channel_id=1, source_target_pairs={{0,8},{8,16},{16,24},{24,0},{1,9},{9,17},{17,25},{25,1},{2,10},{10... | collective-permute-start | bytes 786440 | tf_op jit(solution)/shard_map/ppermute | solution.py:16
  91.7 0.6 dynamic_slice.15
  92.2 0.6 iota_compare_fusion
  92.9 5.2 %collective-permute-done.2 = bf16[128,1024]{1,0:T(8,128)(2,1)S(1)} collective-permute-done((bf16[128,1024]{1,0:T(8,128)(2,1)S(1)}, bf16[128,1024]{1,0:T(8,128)(2,1)S(1)}, u32[]{:S(2)}, u32[]{:S(2)}) %collective-permute-start.2) | collective-permute-done | bytes 262176 | tf_op jit(solution)/shard_map/ppermute | solution.py:16
  98.1 0.0 collective-permute-start.3
  98.1 0.7 broadcast_compare_fusion.1
  98.8 0.9 copy.25
  99.6 3.8 %collective-permute-start.4 = (bf16[128,1024]{1,0:T(8,128)(2,1)}, bf16[128,1024]{1,0:T(8,128)(2,1)S(1)}, u32[]{:S(2)}, u32[]{:S(2)}) collective-permute-start(bf16[128,1024]{1,0:T(8,128)(2,1)} %copy-done.5), channel_id=1, source_target_pairs={{0,24},{8,0},{16,8},{24,16},{1,25},{9,1},{17,9},{25,17},{2,26},{10... | collective-permute-start | bytes 786440 | tf_op jit(solution)/shard_map/ppermute | solution.py:18
  103.4 1.0 convolution_convert_fusion
  104.4 1.0 copy.22
  105.4 2.7 %collective-permute-done.3 = bf16[128,1024]{1,0:T(8,128)(2,1)S(1)} collective-permute-done((bf16[128,1024]{1,0:T(8,128)(2,1)S(1)}, bf16[128,1024]{1,0:T(8,128)(2,1)S(1)}, u32[]{:S(2)}, u32[]{:S(2)}) %collective-permute-start.3) | collective-permute-done | bytes 262176 | tf_op jit(solution)/shard_map/ppermute | solution.py:16
  108.2 2.5 %collective-permute-done.4 = bf16[128,1024]{1,0:T(8,128)(2,1)S(1)} collective-permute-done((bf16[128,1024]{1,0:T(8,128)(2,1)}, bf16[128,1024]{1,0:T(8,128)(2,1)S(1)}, u32[]{:S(2)}, u32[]{:S(2)}) %collective-permute-start.4) | collective-permute-done | bytes 262176 | tf_op jit(solution)/shard_map/ppermute | solution.py:18
  110.8 0.9 constant_dynamic-slice_fusion
  111.7 1.0 copy.21
  112.7 1.7 %bitcast_reduce_fusion = (f32[128,8]{0,1:T(8,128)S(1)}, f32[8,512,128]{2,1,0:T(8,128)S(1)}) fusion(pred[512]{0:T(512)(128)(4,1)S(1)} %iota_compare_fusion, bf16[512,8,64]{0,2,1:T(8,128)(2,1)} %bitcast.63, bf16[128,8,64]{0,2,1:T(8,128)(2,1)S(1)} %bitcast.64), kind=kOutput, calls=%fused_computation.1 | convolution fusion | flops 68680704 | bytes 2757120 | tf_op jit(solution)/shard_map/while/body/eval_jaxpr/fhd,nhd->fhn/dot_general | solution.py:43
  114.4 0.6 fusion.2
  115.0 2.0 %copy.23 = bf16[512,512]{0,1:T(8,128)(2,1)} copy(bf16[512,512]{1,0:T(8,128)(2,1)} %get-tuple-element.23) | data formatting | bytes 1048576 | tf_op jit(solution)/shard_map/slice | solution.py:131
  117.0 1.8 %fusion.7 = bf16[128,8,64]{0,2,1:T(8,128)(2,1)S(1)} fusion(bf16[512,8,64]{0,2,1:T(8,128)(2,1)} %bitcast.65, f32[8,512,128]{2,1,0:T(8,128)S(1)} %get-tuple-element.37, f32[128,8]{0,1:T(8,128)S(1)} %broadcast_maximum_fusion, pred[512]{0:T(512)(128)(4,1)S(1)} %iota_compare_fusion, f32[128,8]{0,1:T(8,128)S(1)} %get-tuple-element.35, ...), kind=kOutput, calls=%fused_computation.11 | convolution fusion | flops 69992448 | bytes 2765440 | tf_op jit(solution)/shard_map/while/body/eval_jaxpr/fhn,nhd->fhd/dot_general | solution.py:52
  118.8 0.8 copy.26
  (32 shorter events, 0.3 us)
Async XLA Ops:
  0.6 87.6 %copy-start = (bf16[1024,512]{1,0:T(8,128)(2,1)S(1)}, bf16[1024,512]{1,0:T(8,128)(2,1)}, u32[]{:S(2)}) copy-start(bf16[1024,512]{1,0:T(8,128)(2,1)} %param.17) | copy-start | bytes 3145732
  1.9 31.7 %copy-start.1 = (bf16[2,128,512]{1,2,0:T(8,128)(2,1)}, bf16[2,128,512]{1,2,0:T(8,128)(2,1)S(1)}, u32[]{:S(2)}) copy-start(bf16[2,128,512]{1,2,0:T(8,128)(2,1)S(1)} %copy.17) | copy-start | bytes 786436
  2.6 0.6 copy-start.9
  3.4 30.8 %collective-permute-start = (bf16[2,64,512]{1,2,0:T(8,128)(2,1)S(1)}, bf16[2,64,512]{1,2,0:T(8,128)(2,1)S(1)}, u32[]{:S(2)}, u32[]{:S(2)}) collective-permute-start(bf16[2,64,512]{1,2,0:T(8,128)(2,1)S(1)} %get-tuple-element.32), channel_id=1, source_target_pairs={{0,8},{8,16},{16,24},{1,9},{9,17},{17,25},{2,10},{10,18},{18,26},{... | collective-permute-start | bytes 393224 | tf_op jit(solution)/shard_map/ppermute | solution.py:30
  8.3 25.3 %copy-start.11 = (bf16[512]{0:T(512)(128)(2,1)S(1)}, bf16[512]{0:T(512)(128)(2,1)}, u32[]{:S(2)}) copy-start(bf16[512]{0:T(512)(128)(2,1)} %param.12) | copy-start | bytes 3076
  8.3 25.8 %collective-permute-start.1 = (bf16[2,64,512]{1,2,0:T(8,128)(2,1)S(1)}, bf16[2,64,512]{1,2,0:T(8,128)(2,1)S(1)}, u32[]{:S(2)}, u32[]{:S(2)}) collective-permute-start(bf16[2,64,512]{1,2,0:T(8,128)(2,1)S(1)} %get-tuple-element.33), channel_id=1, source_target_pairs={{8,0},{16,8},{24,16},{9,1},{17,9},{25,17},{10,2},{18,10},{26,18},{... | collective-permute-start | bytes 393224 | tf_op jit(solution)/shard_map/ppermute | solution.py:31
  36.6 41.8 %copy-start.2 = (bf16[2,128,512]{1,2,0:T(8,128)(2,1)S(1)}, bf16[2,128,512]{1,2,0:T(8,128)(2,1)}, u32[]{:S(2)}) copy-start(bf16[2,128,512]{1,2,0:T(8,128)(2,1)} %copy-done.1) | copy-start | bytes 786436
  36.6 41.8 %copy-start.6 = (f32[512]{0:T(512)S(1)}, f32[512]{0:T(512)}, u32[]{:S(2)}) copy-start(f32[512]{0:T(512)} %convert_element_type.59) | copy-start | bytes 6148
  36.6 41.9 %copy-start.10 = (pred[2,128]{1,0:T(4,128)(4,1)S(1)}, pred[2,128]{1,0:T(4,128)(4,1)}, u32[]{:S(2)}) copy-start(pred[2,128]{1,0:T(4,128)(4,1)} %copy-done.9) | copy-start | bytes 772
  77.7 10.2 %copy-start.7 = (f32[1024]{0:T(1024)S(1)}, f32[1024]{0:T(1024)}, u32[]{:S(2)}) copy-start(f32[1024]{0:T(1024)} %param.14) | copy-start | bytes 12292
  77.7 10.1 %copy-start.8 = (f32[1024]{0:T(1024)S(1)}, f32[1024]{0:T(1024)}, u32[]{:S(2)}) copy-start(f32[1024]{0:T(1024)} %param.13) | copy-start | bytes 12292
  78.5 10.1 %copy-start.3 = (bf16[1024,512]{1,0:T(8,128)(2,1)S(1)}, bf16[1024,512]{1,0:T(8,128)(2,1)}, u32[]{:S(2)}) copy-start(bf16[1024,512]{1,0:T(8,128)(2,1)} %param.16) | copy-start | bytes 3145732
  87.7 4.0 %copy-start.12 = (s32[2]{0:T(128)S(1)}, s32[2]{0:T(128)}, u32[]{:S(2)}) copy-start(s32[2]{0:T(128)} %param.10) | copy-start | bytes 28
  88.2 15.2 %copy-start.4 = (bf16[1024,512]{1,0:T(8,128)(2,1)S(1)}, bf16[1024,512]{1,0:T(8,128)(2,1)}, u32[]{:S(2)}) copy-start(bf16[1024,512]{1,0:T(8,128)(2,1)} %param.15) | copy-start | bytes 3145732
  88.9 4.0 %copy-start.5 = (bf16[128,1024]{1,0:T(8,128)(2,1)}, bf16[128,1024]{1,0:T(8,128)(2,1)S(1)}, u32[]{:S(2)}) copy-start(bf16[128,1024]{1,0:T(8,128)(2,1)S(1)} %pad_maximum_fusion.2) | copy-start | bytes 786436
  88.9 9.1 %collective-permute-start.2 = (bf16[128,1024]{1,0:T(8,128)(2,1)S(1)}, bf16[128,1024]{1,0:T(8,128)(2,1)S(1)}, u32[]{:S(2)}, u32[]{:S(2)}) collective-permute-start(bf16[128,1024]{1,0:T(8,128)(2,1)S(1)} %pad_maximum_fusion.2), channel_id=1, source_target_pairs={{0,8},{8,16},{16,24},{24,0},{1,9},{9,17},{17,25},{25,1},{2,10},{10... | collective-permute-start | bytes 786440 | tf_op jit(solution)/shard_map/ppermute | solution.py:16
  98.1 10.0 %collective-permute-start.3 = (bf16[128,1024]{1,0:T(8,128)(2,1)S(1)}, bf16[128,1024]{1,0:T(8,128)(2,1)S(1)}, u32[]{:S(2)}, u32[]{:S(2)}) collective-permute-start(bf16[128,1024]{1,0:T(8,128)(2,1)S(1)} %collective-permute-done.2), channel_id=1, source_target_pairs={{0,8},{8,16},{16,24},{24,0},{1,9},{9,17},{17,25},{25,1},{2,10},{10... | collective-permute-start | bytes 786440 | tf_op jit(solution)/shard_map/ppermute | solution.py:16
  99.6 11.1 %collective-permute-start.4 = (bf16[128,1024]{1,0:T(8,128)(2,1)}, bf16[128,1024]{1,0:T(8,128)(2,1)S(1)}, u32[]{:S(2)}, u32[]{:S(2)}) collective-permute-start(bf16[128,1024]{1,0:T(8,128)(2,1)} %copy-done.5), channel_id=1, source_target_pairs={{0,24},{8,0},{16,8},{24,16},{1,25},{9,1},{17,9},{25,17},{2,26},{10... | collective-permute-start | bytes 786440 | tf_op jit(solution)/shard_map/ppermute | solution.py:18
